TPU v7x, 32 devices: a whole 2x2x4 slice. The times are simulated.
32 devices in a mesh: fsdp: 16 (over z, x, core), tp: 2 (over y).
Axes of the slice: x: 2, y: 2, z: 4, core: 2. Of those that a mesh axis runs over, the one named last changes fastest.
Arguments:
- xbc: bfloat16 [4096, 8, 2304], P('fsdp', 'tp'), may hold values from -6 to 6
- dt_raw: bfloat16 [256, 4096], P('tp', 'fsdp'), may hold values from -3 to 3
- conv_weight: bfloat16 [4, 8, 2304], P(None, 'tp'), may hold values from -3 to 3
- conv_bias: bfloat16 [8, 2304], P('tp'), may hold values from -3 to 3
- dt_bias: float32 [256], P('tp'), may hold values from -13 to 0
- a_log: float32 [256], P('tp'), may hold values from -1.5 to -0.1
- d_skip: float32 [256], P('tp'), may hold values from 0.5 to 1.5
Outputs:
- mixed: float32 [4096, 16384], P(('fsdp', 'tp'))
All inputs are finite; a program needn't handle non-finite values.
Results may differ from a plain program's by a relative error of at most 0.0016.
Values may be sent and summed in bfloat16 or wider, within the bound.
No kernel may reach another device: no remote copies, remote signals or barrier semaphores. Data moves between devices by JAX's collectives and lax.ppermute only.
A program may use at most 256 MiB of HBM per device.

v0:
```python
import jax
import jax.numpy as jnp
from jax import lax
from jax.sharding import PartitionSpec as P

HEAD_DIM = 64
STATE = 128


def from_behind(value, axis, steps):
    count = lax.axis_size(axis)
    initial, last = (max(0, -steps), min(count, count - steps))
    return lax.ppermute(value, axis, [(source, source + steps) for source in range(initial, last)])


def carried_in(value, axis, join, neutral):
    count, mine = (lax.axis_size(axis), lax.axis_index(axis))
    pieces = jax.tree.map(lambda part: lax.all_gather(part, axis), value)
    running = jax.tree.map(
        lambda part, zero: jnp.full_like(part, 0) + jnp.asarray(zero, part.dtype), value, neutral
    )

    def step(position, running):
        longer = join(running, jax.tree.map(lambda part: part[position], pieces))
        return jax.tree.map(lambda new, old: jnp.where(position < mine, new, old), longer, running)

    return lax.fori_loop(0, count - 1, step, running)


def convolve(xbc, conv_weight, conv_bias):
    row_count = xbc.shape[0]
    tap_count = conv_weight.shape[0]
    rim_rows = from_behind(xbc[row_count - (tap_count - 1) :], "fsdp", 1)
    padded = jnp.concatenate([rim_rows, xbc], axis=0)
    summed = conv_bias.astype(jnp.float32)[None]
    for k in range(tap_count):
        summed = summed + conv_weight[k].astype(jnp.float32)[None] * padded[
            k : k + row_count
        ].astype(jnp.float32)
    return jax.nn.silu(summed).astype(jnp.bfloat16)


def block_pass(states, pieces, skip_grouped):
    values, b_part, c_part, step_blk, rate_blk = pieces
    block_rows = values.shape[0]
    exact = lax.Precision.HIGHEST
    scores = jnp.einsum("tgn,sgn->gts", c_part, b_part, preferred_element_type=jnp.float32)
    cum_log = jnp.cumsum(rate_blk, axis=2)
    causal = lax.broadcasted_iota(jnp.int32, (block_rows, block_rows), 0) >= lax.broadcasted_iota(
        jnp.int32, (block_rows, block_rows), 1
    )
    gaps = cum_log[:, :, :, None] - cum_log[:, :, None, :]
    decays = jnp.exp(jnp.where(causal, gaps, -jnp.inf))
    mixing = decays * scores[:, None] * step_blk[:, :, None, :]
    output = jnp.einsum("gjts,sgjp->tgjp", mixing, values, precision=exact)
    carried = jnp.einsum("tgn,gjnp->tgjp", c_part.astype(jnp.float32), states, precision=exact)
    output = output + jnp.transpose(jnp.exp(cum_log), (2, 0, 1))[..., None] * carried
    output = output + skip_grouped[None, :, :, None] * values
    ending = cum_log[:, :, -1:]
    weights = jnp.exp(ending - cum_log) * step_blk
    weighted = values * jnp.transpose(weights, (2, 0, 1))[..., None]
    added = jnp.einsum("sgn,sgjp->gjnp", b_part.astype(jnp.float32), weighted, precision=exact)
    states = jnp.exp(ending)[..., None] * states + added
    return (states, output)


def carry_in(decays, states):
    flat_state = states.reshape(decays.shape[0] * decays.shape[1], -1)
    rates = decays.reshape(-1)

    def combine(earlier, latter):
        return (earlier[0] * latter[0], latter[0][:, None] * earlier[1] + latter[1])

    identity = (jnp.ones_like(rates), jnp.zeros_like(flat_state))
    moved = carried_in((rates, flat_state), "fsdp", combine, identity)
    return moved[1].reshape(states.shape)


def shards(xbc, dt_raw, conv_weight, conv_bias, dt_bias, a_log, d_skip):
    row_count, group_count, channel_count = xbc.shape
    head_count = dt_raw.shape[0]
    per_group = head_count // group_count
    inner_width = per_group * HEAD_DIM
    exact = lax.Precision.HIGHEST
    activated = convolve(xbc, conv_weight, conv_bias)
    values = (
        activated[:, :, :inner_width]
        .astype(jnp.float32)
        .reshape(row_count, group_count, per_group, HEAD_DIM)
    )
    b_part = activated[:, :, inner_width : inner_width + STATE]
    c_part = activated[:, :, inner_width + STATE :]
    step_sizes = jax.nn.softplus(dt_raw.astype(jnp.float32) + dt_bias[:, None])
    log_rates = -jnp.exp(a_log)[:, None] * step_sizes
    step_grouped = step_sizes.reshape(group_count, per_group, row_count)
    rate_grouped = log_rates.reshape(group_count, per_group, row_count)
    skip_grouped = d_skip.reshape(group_count, per_group)
    block_rows = min(128, row_count)
    block_count = row_count // block_rows
    pieces = (
        values.reshape(block_count, block_rows, group_count, per_group, HEAD_DIM),
        b_part.reshape(block_count, block_rows, group_count, STATE),
        c_part.reshape(block_count, block_rows, group_count, STATE),
        jnp.moveaxis(step_grouped.reshape(group_count, per_group, block_count, block_rows), 2, 0),
        jnp.moveaxis(rate_grouped.reshape(group_count, per_group, block_count, block_rows), 2, 0),
    )
    cum_device = jnp.cumsum(rate_grouped, axis=2)
    total_decay = jnp.exp(cum_device[:, :, -1])
    zero_state = jnp.zeros((group_count, per_group, STATE, HEAD_DIM), jnp.float32)

    def advance(states, piece):
        return block_pass(states, piece, skip_grouped)

    final_state, block_outputs = lax.scan(advance, zero_state, pieces)
    final_state, partial_value = (
        final_state,
        block_outputs.reshape(row_count, group_count, per_group, HEAD_DIM),
    )
    incoming = carry_in(total_decay, final_state)
    carried = jnp.einsum("tgn,gjnp->tgjp", c_part.astype(jnp.float32), incoming, precision=exact)
    result = partial_value + jnp.transpose(jnp.exp(cum_device), (2, 0, 1))[..., None] * carried
    merged = result.reshape(row_count, head_count * HEAD_DIM)
    return lax.all_to_all(merged, "tp", split_axis=0, concat_axis=1, tiled=True)


def solution(mesh):
    in_specs = (
        P("fsdp", "tp", None),
        P("tp", "fsdp"),
        P(None, "tp", None),
        P("tp", None),
        P("tp"),
        P("tp"),
        P("tp"),
    )
    out_specs = P(("fsdp", "tp"), None)
    return jax.shard_map(shards, mesh=mesh, in_specs=in_specs, out_specs=out_specs, check_vma=False)
```

profile of v0, /device:TPU:24, one launch (start us, length us, event | category | flops | bytes accessed | tf_op | source)
XLA Modules:
  0.0 903.4 jit_solution(15608198483211704366)
XLA Ops:
  6.6 3.0 copy.54
  9.6 2.1 copy-done.2
  11.7 1.9 collective-permute-start
  13.7 0.2 compare_select_fusion
  14.1 4.2 collective-permute-done
  18.3 13.3 %multiply_convert_fusion = bf16[256,4,2304]{2,0,1:T(8,128)(2,1)S(1)} fusion(bf16[256,4,2304]{2,0,1:T(8,128)(2,1)} %copy-done.2, bf16[3,4,2304]{2,0,1:T(4,128)(2,1)S(1)} %collective-permute-done, f32[4,2304]{1,0:T(4,128)S(1)} %get-tuple-element.272, f32[4,2304]{1,0:T(4,128)S(1)} %get-tuple-element.273, f32[4,2304]{1,0:T(4,128)S(1)} %get-tuple-element.271, ...), kind=kLoop, calls=%fused_computation.48 | loop fusion | flops 61341696 | bytes 9676800 | tf_op jit(solution)/shard_map/convert_element_type | solution.py:40
  31.8 2.1 copy-done.1
  33.8 4.4 slice_convert_fusion
  38.2 14.4 %reshape.70 = f32[2,128,4,32,64]{4,3,1,0,2:T(8,128)} reshape(f32[256,4,2048]{2,0,1:T(8,128)} %slice_convert_fusion) | data formatting | bytes 16777216 | tf_op jit(solution)/shard_map/reshape;reshape | solution.py:101
  52.6 14.5 %copy.59 = f32[2,128,4,32,64]{1,4,3,2,0:T(8,128)} copy(f32[2,128,4,32,64]{4,3,1,0,2:T(8,128)} %reshape.70) | data formatting | bytes 16777216
  67.1 251.7 %while.27 = (s32[]{:T(128)}, f32[4,32,128,64]{2,3,1,0:T(8,128)}, f32[2,128,4,32,64]{1,0,4,3,2:T(2,128)}, f32[2,4,32,128]{3,0,2,1:T(2,128)S(1)}, f32[2,128,4,32,6...) while((s32[]{:T(128)}, f32[4,32,128,64]{2,3,1,0:T(8,128)}, ...), condition=%wide.region_2.3_spmd.clone, body=%wide.region_0.2_spmd.clone.sunk | while | flops 4867522560 | bytes 90155176 | solution.py:114
  67.2 0.1 constant_dynamic-slice_fusion.3
  67.3 1.2 reduce_window_sum.33
  68.5 0.2 exponential_reduce_fusion.2
  68.8 0.2 fusion.68
  69.0 0.5 broadcast_select_fusion.2
  69.5 2.4 copy-done
  71.9 3.9 bitcast_add_fusion.4
  75.8 2.2 fusion.67
  78.0 18.1 %fusion.69 = f32[128,4,32,64]{0,3,2,1:T(8,128)} fusion(f32[128,4,32,64]{0,3,2,1:T(8,128)S(1)} %bitcast.153, f32[2,128,4,32,64]{1,4,3,2,0:T(8,128)S(1)} %copy-done, s32[]{:T(128)S(6)} %copy.93, f32[4,32]{1,0:T(4,128)S(1)} %mul.277, f32[128,4,32]{0,2,1:T(8,128)S(1)} %get-tuple-element.368, f32[4,32,128]{2,1,0:T(8,128)S(1)} %bitcast.159, ...), kind=kOutput, calls=%fused_computation.10.clone.1 | convolution fusion | flops 1623195648 | bytes 17320960 | tf_op jit(solution)/shard_map/while/body/eval_jaxpr/gjts,sgjp->tgjp/dot_general | solution.py:55
  96.1 96.2 %dynamic_update_slice.6 = f32[2,128,4,32,64]{1,0,4,3,2:T(2,128)} dynamic-update-slice(f32[2,128,4,32,64]{1,0,4,3,2:T(2,128)} %get-tuple-element.388, f32[1,128,4,32,64]{1,0,4,3,2:T(1,128)} %bitcast.152, s32[]{:T(128)S(6)} %copy.93, s32[]{:T(128)} %constant.58.clone.1..sunk, s32[]{:T(128)} %constant.58.clone.1..sunk, s32[]{:T(128)} %constant.58.clone.1..sunk, s32[]{:T(128)} %constant.58.clone.1..sunk) | dynamic-update-slice | bytes 8388612 | tf_op jit(solution)/shard_map/while/body/jit(dynamic_update_index_in_dim)/dynamic_update_slice | solution.py:114
  192.4 0.1 constant_dynamic-slice_fusion.3
  192.5 1.2 reduce_window_sum.33
  193.7 0.2 exponential_reduce_fusion.2
  194.0 0.2 fusion.68
  194.2 2.9 broadcast_select_fusion.2
  197.1 1.3 copy-done
  198.4 3.9 bitcast_add_fusion.4
  202.3 2.2 fusion.67
  204.5 18.1 %fusion.69 = f32[128,4,32,64]{0,3,2,1:T(8,128)} fusion(f32[128,4,32,64]{0,3,2,1:T(8,128)S(1)} %bitcast.153, f32[2,128,4,32,64]{1,4,3,2,0:T(8,128)S(1)} %copy-done, s32[]{:T(128)S(6)} %copy.93, f32[4,32]{1,0:T(4,128)S(1)} %mul.277, f32[128,4,32]{0,2,1:T(8,128)S(1)} %get-tuple-element.368, f32[4,32,128]{2,1,0:T(8,128)S(1)} %bitcast.159, ...), kind=kOutput, calls=%fused_computation.10.clone.1 | convolution fusion | flops 1623195648 | bytes 17320960 | tf_op jit(solution)/shard_map/while/body/eval_jaxpr/gjts,sgjp->tgjp/dot_general | solution.py:55
  222.6 96.2 %dynamic_update_slice.6 = f32[2,128,4,32,64]{1,0,4,3,2:T(2,128)} dynamic-update-slice(f32[2,128,4,32,64]{1,0,4,3,2:T(2,128)} %get-tuple-element.388, f32[1,128,4,32,64]{1,0,4,3,2:T(1,128)} %bitcast.152, s32[]{:T(128)S(6)} %copy.93, s32[]{:T(128)} %constant.58.clone.1..sunk, s32[]{:T(128)} %constant.58.clone.1..sunk, s32[]{:T(128)} %constant.58.clone.1..sunk, s32[]{:T(128)} %constant.58.clone.1..sunk) | dynamic-update-slice | bytes 8388612 | tf_op jit(solution)/shard_map/while/body/jit(dynamic_update_index_in_dim)/dynamic_update_slice | solution.py:114
  318.8 6.9 copy.68
  325.7 7.9 all_gather_reshape.4
  333.6 2.3 reduce-window.6
  336.0 0.1 slice.69
  336.1 0.1 copy.65
  336.2 0.1 copy_bitcast_fusion
  336.3 0.2 fusion.42
  336.6 16.3 %all-gather = f32[16,1,128]{2,1,0:T(1,128)S(1)} all-gather(f32[1,1,128]{2,1,0:T(1,128)S(1)} %reshape.63), channel_id=1, replica_groups=mesh['fsdp'=16,'tp'=2] {'fsdp'}, dimensions={0}, use_global_device_ids=true | all-gather | bytes 8704 | tf_op jit(solution)/shard_map/all_gather | solution.py:18
  352.9 0.1 exponential_bitcast_fusion.1
  353.0 11.6 %reshape.55 = f32[256,4,32,64]{0,3,2,1:T(8,128)} reshape(f32[2,128,4,32,64]{1,0,4,3,2:T(2,128)} %get-tuple-element.147) | data formatting | bytes 16777216 | tf_op jit(solution)/shard_map/reshape | solution.py:117
  364.6 295.4 %all-gather.3.cloned.1.call-done = f32[16,128,8192]{2,1,0:T(8,128)} async-done(((f32[1,128,8192]{2,1,0:T(8,128)}), f32[16,128,8192]{2,1,0:T(8,128)}) %all-gather.3.cloned.1.call-update) | async-done | bytes 67108880 | tf_op jit(solution)/shard_map/all_gather | solution.py:18
  659.9 92.0 %while.28 = (s32[]{:T(128)}, f32[128,8192]{1,0:T(8,128)}, s32[]{:T(128)}, f32[16,128]{1,0:T(8,128)S(1)}, f32[16,128,8192]{2,1,0:T(8,128)}, /*index=5*/s32[]{:T(128)}, s32[]{:T(128)}) while((s32[]{:T(128)}, f32[128,8192]{1,0:T(8,128)}, s32[]{:T(128)}, f32[16,128]{1,0:T(8,128)S(1)}, f32[16,128,8192]{2,1,0:T(8,128)}, ...), condition=%wide.region_6.7_spmd.clone, body=%wide.region_5.6_spmd.clone.sunk | while | flops 4194308 | bytes 12584561 | solution.py:27
  660.0 4.9 fusion.70
  664.9 6.2 fusion.70
  671.1 6.2 fusion.70
  677.3 6.2 fusion.70
  683.6 6.2 fusion.70
  689.8 6.2 fusion.70
  696.0 6.2 fusion.70
  702.2 6.2 fusion.70
  708.4 6.2 fusion.70
  714.7 6.2 fusion.70
  720.9 6.2 fusion.70
  727.1 6.2 fusion.70
  733.3 6.2 fusion.70
  739.5 6.2 fusion.70
  745.8 6.2 fusion.70
  752.0 7.8 reshape.57
  759.8 15.8 %fusion.38 = f32[256,4,32,64]{0,3,2,1:T(8,128)} fusion(f32[256,4,32,64]{0,3,2,1:T(8,128)} %reshape.55, f32[256,4,32]{0,2,1:T(8,128)S(1)} %exponential_bitcast_fusion.1, f32[4,32,128,64]{3,2,1,0:T(8,128)} %reshape.57, bf16[256,4,2304]{2,0,1:T(8,128)(2,1)} %copy-done.1), kind=kOutput, calls=%fused_computation.50 | convolution fusion | flops 3225419776 | bytes 25559040 | tf_op jit(solution)/shard_map/tgn,gjnp->tgjp/dot_general | solution.py:120
  775.6 10.8 %all_to_all.14 = f32[2,128,8192]{1,0,2:T(2,128)} reshape(f32[256,4,32,64]{0,3,2,1:T(8,128)} %fusion.38) | data formatting | bytes 16777216 | tf_op jit(solution)/shard_map/all_to_all | solution.py:123
  786.4 3.9 copy.70
  790.3 97.3 %all_to_all.19 = f32[2,128,8192]{1,2,0:T(8,128)} all-to-all(f32[2,128,8192]{1,2,0:T(8,128)S(1)} %copy.70), channel_id=1, replica_groups=mesh['fsdp'=16,'tp'=2] {'tp'}, dimensions={0} | all-to-all | bytes 16777216 | tf_op jit(solution)/shard_map/all_to_all | solution.py:123
  887.6 9.0 copy.71
  (54 shorter events, 1.0 us)
Async XLA Ops:
  6.5 7.1 copy-start.8
  6.5 7.1 copy-start.3
  6.5 7.2 copy-start.7
  6.5 7.2 copy-start.4
  6.5 7.4 copy-start.5
  6.5 653.4 %all-gather.3.cloned.1.call-start = ((), (), s32[]{:S(2)}) async-start(), calls=%async_computation.1 | async-start | bytes 71303168 | tf_op jit(solution)/shard_map/all_gather | solution.py:18
  9.6 2.1 copy-start.2
  11.7 6.6 collective-permute-start
  31.6 2.2 copy-start.1
  52.6 14.5 %copy-start.6 = (f32[128]{0:T(128)S(1)}, f32[128]{0:T(128)}, u32[]{:S(2)}) copy-start(f32[128]{0:T(128)} %param.17) | copy-start | bytes 1540
  68.5 3.4 copy-start
  193.7 4.7 copy-start
Sparse Core Ops, SparseCore 0:
  333.7 326.1 all-gather.2
where the time goes:
time: 920 us; the launch traced here: 903 us
  waiting for transfers between devices  300 us (33%)
  local copies, waits for them, and re-layouts  292 us (32%)
  other arithmetic  118 us (13%)
  blocking collectives  114 us (12%)
  matrix products  64.6 us (7%)
  between operations  13.6 us (1%)
    all_gather x1, waiting for transfers between devices, carried_in(): pieces = jax.tree.map(lambda part: lax.all_gather(part, axis), value)  295 us
    dynamic_update_slice x2, local copies, waits for them, and re-layouts, shards(): final_state, block_outputs = lax.scan(advance, zero_state, pieces)  192 us
    all_to_all x1, blocking collectives, shards(): return lax.all_to_all(merged, 'tp', split_axis=0, concat_axis=1, tiled=True)  97.3 us
    select_n x15, other arithmetic, step(): jnp.where(position < mine, new, old)  91.9 us
    dot_general x2, matrix products, block_pass(): output = jnp.einsum('gjts,sgjp->tgjp', mixing, values, precision=exact)  36.2 us
    all_to_all x3, local copies, waits for them, and re-layouts, shards(): return lax.all_to_all(merged, 'tp', split_axis=0, concat_axis=1, tiled=True)  23.7 us
    unnamed x19, local copies, waits for them, and re-layouts  21.7 us
  transfers between devices with their start and end apart: 2, of which 2 were waited for; matrix products, arithmetic and copies ran while one was open for 2% of the time, Pallas kernels for 0%

commit v1 on v0

v1 whole, which is shorter than its diff:
```python
import jax
import jax.numpy as jnp
from jax import lax
from jax.sharding import Mesh, PartitionSpec as P

HEAD_DIM = 64
STATE = 128
SEQ = ("fh", "fl")


def convolve(xbc, conv_weight, conv_bias, seq_count):
    row_count = xbc.shape[0]
    tap_count = conv_weight.shape[0]
    rim = xbc[row_count - (tap_count - 1) :]
    rim_rows = lax.ppermute(rim, SEQ, [(d, d + 1) for d in range(seq_count - 1)])
    padded = jnp.concatenate([rim_rows, xbc], axis=0)
    summed = conv_bias.astype(jnp.float32)[None]
    for k in range(tap_count):
        summed = summed + conv_weight[k].astype(jnp.float32)[None] * padded[
            k : k + row_count
        ].astype(jnp.float32)
    return jax.nn.silu(summed).astype(jnp.bfloat16)


def shards(xbc, dt_raw, conv_weight, conv_bias, dt_bias, a_log, d_skip, seq_count):
    row_count, group_count, _ = xbc.shape
    head_count = dt_raw.shape[0]
    per_group = head_count // group_count
    inner_width = per_group * HEAD_DIM
    exact = lax.Precision.HIGHEST
    f32 = jnp.float32

    activated = convolve(xbc, conv_weight, conv_bias, seq_count)
    chunk = min(128, row_count)
    nck = row_count // chunk
    values = activated[:, :, :inner_width].reshape(nck, chunk, group_count, per_group, HEAD_DIM)
    b_part = activated[:, :, inner_width : inner_width + STATE].reshape(nck, chunk, group_count, STATE)
    c_part = activated[:, :, inner_width + STATE :].reshape(nck, chunk, group_count, STATE)

    step_sizes = jax.nn.softplus(dt_raw.astype(f32) + dt_bias[:, None])
    log_rates = -jnp.exp(a_log)[:, None] * step_sizes
    steps = step_sizes.reshape(group_count, per_group, nck, chunk)
    rates = log_rates.reshape(group_count, per_group, nck, chunk)
    cum = jnp.cumsum(rates, axis=3)
    chunk_log = cum[..., -1]

    causal = lax.broadcasted_iota(jnp.int32, (chunk, chunk), 0) >= lax.broadcasted_iota(
        jnp.int32, (chunk, chunk), 1
    )
    scores = jnp.einsum("ktgn,ksgn->kgts", c_part, b_part, preferred_element_type=f32)
    gaps = cum[..., :, None] - cum[..., None, :]
    decays = jnp.exp(jnp.where(causal, gaps, -jnp.inf))
    mixing = decays * jnp.transpose(scores, (1, 0, 2, 3))[:, None] * steps[..., None, :]
    values32 = values.astype(f32)
    output = jnp.einsum("gjkts,ksgjp->ktgjp", mixing, values32, precision=exact)
    output = output + d_skip.reshape(group_count, per_group)[None, None, :, :, None] * values32

    weights = jnp.exp(chunk_log[..., None] - cum) * steps
    weighted = values32 * jnp.transpose(weights, (2, 3, 0, 1))[..., None]
    chunk_states = jnp.einsum("ksgn,ksgjp->kgjnp", b_part.astype(f32), weighted, precision=exact)

    kk = jnp.arange(nck)
    between = (kk[None, :, None] < kk[None, None, :]) & (kk[None, None, :] < kk[:, None, None])
    gap_log = jnp.einsum("kam,gjm->gjka", between.astype(f32), chunk_log)
    pre_w = jnp.where((kk[None, :] < kk[:, None])[None, None], jnp.exp(gap_log), 0.0)
    local_in = jnp.einsum("gjka,agjnp->kgjnp", pre_w, chunk_states, precision=exact)
    cum_dev = cum + jnp.concatenate(
        [jnp.zeros_like(chunk_log[..., :1]), jnp.cumsum(chunk_log, axis=2)[..., :-1]], axis=2
    )[..., None]
    dev_log = jnp.sum(chunk_log, axis=2)
    later = (kk[:, None] < kk[None, :]).astype(f32)
    after_w = jnp.exp(jnp.einsum("km,gjm->gjk", later, chunk_log))
    dev_state = jnp.einsum("gjk,kgjnp->gjnp", after_w, chunk_states, precision=exact)

    carried_local = jnp.einsum("ktgn,kgjnp->ktgjp", c_part.astype(f32), local_in, precision=exact)
    output = output + jnp.transpose(jnp.exp(cum), (2, 3, 0, 1))[..., None] * carried_local

    lo = lax.axis_index("fl")
    hi = lax.axis_index("fh")
    pair_count = seq_count // 2
    half = per_group // 2
    all_log = lax.all_gather(dev_log, SEQ)
    first_log = all_log[2 * hi]
    second_log = all_log[2 * hi + 1]
    own_half = lax.dynamic_slice_in_dim(dev_state, lo * half, half, axis=1)
    other_half = lax.dynamic_slice_in_dim(dev_state, (1 - lo) * half, half, axis=1)
    swap = [(0, 1), (1, 0)]
    recv_a = lax.ppermute(other_half, "fl", swap)
    first_state = jnp.where(lo == 0, own_half, recv_a)
    second_state = jnp.where(lo == 0, recv_a, own_half)
    second_log_half = lax.dynamic_slice_in_dim(second_log, lo * half, half, axis=1)
    first_log_half = lax.dynamic_slice_in_dim(first_log, lo * half, half, axis=1)
    pair_state = jnp.exp(second_log_half)[..., None, None] * first_state + second_state
    gathered = lax.all_gather(pair_state, "fh")

    pair_log = all_log.reshape(pair_count, 2, group_count, per_group).sum(axis=1)
    pair_log_half = lax.dynamic_slice_in_dim(pair_log, lo * half, half, axis=2)
    pp = jnp.arange(pair_count)
    strictly = (pp[:, None] < pp[None, :]) & (pp[None, :] < hi)
    gap = jnp.einsum("am,mgj->agj", strictly.astype(f32), pair_log_half)
    pair_w = jnp.where((pp < hi)[:, None, None], jnp.exp(gap), 0.0)
    pair_in = jnp.einsum("agj,agjnp->gjnp", pair_w, gathered, precision=exact)

    first_decay = jnp.exp(first_log_half)[..., None, None]
    own_in = jnp.where(lo == 0, pair_in, first_decay * pair_in + recv_a)
    sent = jnp.where(lo == 0, first_decay * pair_in + own_half, pair_in)
    recv_c = lax.ppermute(sent, "fl", swap)
    incoming = jnp.where(
        lo == 0,
        jnp.concatenate([own_in, recv_c], axis=1),
        jnp.concatenate([recv_c, own_in], axis=1),
    )

    carried = jnp.einsum("ktgn,gjnp->ktgjp", c_part.astype(f32), incoming, precision=exact)
    output = output + jnp.transpose(jnp.exp(cum_dev), (2, 3, 0, 1))[..., None] * carried
    merged = output.reshape(row_count, head_count * HEAD_DIM)
    return lax.all_to_all(merged, "tp", split_axis=0, concat_axis=1, tiled=True)


def solution(mesh):
    seq_count = mesh.shape["fsdp"]
    tp_count = mesh.shape["tp"]
    grid = Mesh(mesh.devices.reshape(seq_count // 2, 2, tp_count), ("fh", "fl", "tp"))
    in_specs = (
        P(SEQ, "tp", None),
        P("tp", SEQ),
        P(None, "tp", None),
        P("tp", None),
        P("tp"),
        P("tp"),
        P("tp"),
    )
    out_specs = P(SEQ + ("tp",), None)

    def body(*args):
        return shards(*args, seq_count=seq_count)

    return jax.shard_map(body, mesh=grid, in_specs=in_specs, out_specs=out_specs, check_vma=False)
```

time: 920 us -> 535 us (0.58); the launches traced: 903 us -> 530 us
  local copies, waits for them, and re-layouts: 292 us -> 45.3 us
  other arithmetic: 118 us -> 32.3 us
  waiting for transfers between devices: 300 us -> 228 us
  matrix products: 64.6 us -> 88.2 us
    dynamic_update_slice x2 -> x0, local copies, waits for them, and re-layouts: 192 us -> none  [shards(): final_state, block_outputs = lax.scan(advance, zero_state, pieces)]
    select_n x16 -> x2, other arithmetic: 92.1 us -> 3.48 us  [the longest x1 3.33 us: shards(): own_in = jnp.where(lo == 0, pair_in, first_decay * pair_in + recv_a)]
    all_gather x1, waiting for transfers between devices: 295 us -> 227 us  [shards(): gathered = lax.all_gather(pair_state, 'fh')]
    dot_general x7 -> x9, matrix products: 60.2 us -> 88.2 us  [the longest x1 37.9 us: shards(): jnp.einsum('gjka,agjnp->kgjnp', pre_w, chunk_states, precision=exact)]
    another operation x7 -> x0, local copies, waits for them, and re-layouts: 22.5 us -> none  [the longest x1 14.4 us: shards(): values.reshape(block_count, block_rows, group_count, per_group, HEAD_DIM)]
    all_to_all x3 -> x1, local copies, waits for them, and re-layouts: 23.7 us -> 8.99 us  [shards(): return lax.all_to_all(merged, 'tp', split_axis=0, concat_axis=1, tiled=True)]
    unnamed x19 -> x23, local copies, waits for them, and re-layouts: 21.7 us -> 7.17 us
    while x5 -> x0, local copies, waits for them, and re-layouts: 10.6 us -> none  [the longest x1 6.9 us: shards(): final_state, block_outputs = lax.scan(advance, zero_state, pieces)]
  transfers between devices with their start and end apart: 2 -> 4, of which waited for: 2 -> 2; matrix products, arithmetic and copies ran while one was open for 2% -> 13% of each run, Pallas kernels for 0% -> 0%
where the time goes in v1:
time: 535 us; the launch traced here: 530 us
  waiting for transfers between devices  228 us (43%)
  blocking collectives  120 us (22%)
  matrix products  88.2 us (16%)
  local copies, waits for them, and re-layouts  45.3 us (8%)
  other arithmetic  32.3 us (6%)
  between operations  13.7 us (3%)
    all_gather x1, waiting for transfers between devices, shards(): gathered = lax.all_gather(pair_state, 'fh')  227 us
    all_to_all x1, blocking collectives, shards(): return lax.all_to_all(merged, 'tp', split_axis=0, concat_axis=1, tiled=True)  104 us
    dot_general x1, matrix products, shards(): jnp.einsum('gjka,agjnp->kgjnp', pre_w, chunk_states, precision=exact)  37.9 us
    reshape x2, local copies, waits for them, and re-layouts, shards(): activated[:, :, :inner_width]  24.3 us
    dot_general x1, matrix products, shards(): output = jnp.einsum('gjkts,ksgjp->ktgjp', mixing, values32, precision=exact)  19.8 us
    all_gather x1, blocking collectives, shards(): all_log = lax.all_gather(dev_log, SEQ)  15.8 us
    dot_general x1, matrix products, shards(): jnp.einsum('ktgn,gjnp->ktgjp', c_part.astype(f32), incoming, precision=ex...  14.2 us
    convert_element_type x1, other arithmetic, convolve(): return jax.nn.silu(summed).astype(jnp.bfloat16)  13.6 us
  transfers between devices with their start and end apart: 4, of which 2 were waited for; matrix products, arithmetic and copies ran while one was open for 13% of the time, Pallas kernels for 0%

profile of v1, /device:TPU:24, one launch (start us, length us, event | category | flops | bytes accessed | tf_op | source)
XLA Modules:
  0.0 529.7 jit_solution(4426078472640493439)
XLA Ops:
  6.5 0.0 copy-start.4
  6.5 0.0 copy-start.9
  6.5 0.0 copy-start.7
  6.5 0.0 copy-start.5
  6.5 0.0 copy-start.6
  6.5 0.0 all-gather.5.cloned.1.call-start
  6.6 3.0 copy.67
  9.6 0.0 copy-start.2
  9.6 2.2 copy-done.2
  11.8 1.9 collective-permute-start
  13.7 0.0 copy-done.4
  13.8 0.0 copy-done.9
  13.8 0.0 copy-done.7
  13.8 0.0 copy-done.5
  13.8 0.2 compare_select_fusion
  14.0 0.1 reshape.99
  14.0 2.3 reduce_window_sum.24
  16.4 0.2 slice_reduce_fusion
  16.6 0.1 copy.80
  16.7 0.1 mul.173
  16.8 0.1 fusion.48
  16.9 0.1 convolution_exponential_fusion.2
  17.0 0.0 copy-done.6
  17.0 1.3 collective-permute-done
  18.4 13.6 %multiply_convert_fusion = bf16[256,4,2304]{2,0,1:T(8,128)(2,1)S(1)} fusion(bf16[256,4,2304]{2,0,1:T(8,128)(2,1)} %copy-done.2, bf16[3,4,2304]{2,0,1:T(4,128)(2,1)S(1)} %collective-permute-done, f32[4,2304]{1,0:T(4,128)S(1)} %get-tuple-element.15, f32[4,2304]{1,0:T(4,128)S(1)} %get-tuple-element.16, f32[4,2304]{1,0:T(4,128)S(1)} %get-tuple-element.14, ...), kind=kLoop, calls=%fused_computation.9 | loop fusion | flops 61341696 | bytes 9676800 | tf_op jit(solution)/shard_map/convert_element_type | solution.py:22
  32.0 2.5 slice.57
  34.5 0.1 fusion.63
  34.6 12.9 %reshape.128 = bf16[2,128,4,32,64]{4,3,1,0,2:T(8,128)(2,1)} reshape(bf16[256,4,2048]{2,0,1:T(8,128)(2,1)} %slice.57) | data formatting | bytes 8388608 | tf_op jit(solution)/shard_map/reshape | solution.py:36
  47.5 11.4 %copy.77 = bf16[2,128,4,32,64]{1,4,3,2,0:T(8,128)(2,1)} copy(bf16[2,128,4,32,64]{4,3,1,0,2:T(8,128)(2,1)} %reshape.128) | data formatting | bytes 8388608 | tf_op jit(solution)/shard_map/reshape | solution.py:36
  58.9 9.5 %fusion.10 = (f32[4,32,128,64]{2,3,1,0:T(8,128)S(1)}, f32[2,4,32,64,128]{4,3,2,1,0:T(8,128)}) fusion(f32[4,32,2]{1,0,2:T(4,128)S(1)} %copy.128, bf16[2,128,4,128,1]{3,1,0,2,4:T(8,128)(2,1)S(1)} %bitcast.97, bf16[2,128,4,32,64]{1,4,3,2,0:T(8,128)(2,1)} %copy.77, f32[2,128,4,32]{1,3,0,2:T(8,128)S(1)} %fusion.48), kind=kOutput, calls=%fused_computation.16 | convolution fusion | flops 3228565504 | bytes 17171456 | tf_op jit(solution)/shard_map/ksgn,ksgjp->kgjnp/dot_general | solution.py:60
  68.4 0.0 copy-start.1
  68.4 0.0 copy-start.8
  68.4 2.0 copy-done.1
  70.4 1.5 constant_dynamic-slice_fusion
  71.9 0.3 collective-permute-start.1
  72.2 15.8 %all-gather.2 = f32[16,4,32]{2,1,0:T(4,128)S(1)} all-gather(f32[1,4,32]{2,1,0:T(4,128)S(1)} %bitcast.101), channel_id=2, replica_groups=mesh['fh'=8,'fl'=2,'tp'=2] {'fh','fl'}, dimensions={0}, use_global_device_ids=true | all-gather | bytes 8704 | tf_op jit(solution)/shard_map/all_gather | solution.py:82
  88.0 0.1 exponential_bitcast_fusion
  88.1 0.0 collective-permute-done.1
  88.1 0.0 copy-start.3
  88.1 4.1 select_add_fusion
  92.2 0.0 all-gather.5.cloned.1.call-update
  92.2 0.1 constant_dynamic-slice_fusion.1
  92.3 0.1 fusion.39
  92.5 0.1 fusion.41
  92.6 0.1 copy.98
  92.8 0.0 copy-done.8
  92.8 0.1 mul.176
  92.9 0.1 bitcast_exponential_fusion
  93.0 226.5 %all-gather.5.cloned.1.call-done = f32[32,16,128,64]{2,3,1,0:T(8,128)} async-done(((f32[4,16,128,64]{2,3,1,0:T(8,128)}), f32[32,16,128,64]{2,3,1,0:T(8,128)}) %all-gather.5.cloned.1.call-update) | async-done | bytes 16777232 | tf_op jit(solution)/shard_map/all_gather | solution.py:94
  319.5 8.4 %multiply_reduce_fusion = f32[4,16,128,64]{2,3,1,0:T(8,128)} fusion(f32[4,16,8,128,64]{3,4,1,0,2:T(8,128)} %bitcast.93, f32[4,16,8]{1,0,2:T(4,128)S(1)} %copy.127), kind=kLoop, calls=%fused_computation | loop fusion | flops 7864320 | bytes 18876416 | tf_op jit(solution)/shard_map/agj,agjnp->gjnp/dot_general | solution.py:102
  327.9 0.0 copy-done.3
  327.9 3.3 add_select_fusion.1
  331.3 0.1 collective-permute-start.2
  331.3 37.9 %fusion.21 = f32[2,4,32,128,64]{3,0,4,2,1:T(2,128)S(1)} fusion(f32[4,32,2,2,1]{3,2,4,1,0:T(2,128)S(1)} %copy.98, f32[2,4,32,128,64]{3,4,2,1,0:T(8,128)} %bitcast.90), kind=kOutput, calls=%fused_computation.30 | convolution fusion | flops 50331648 | bytes 16779264 | tf_op jit(solution)/shard_map/gjka,agjnp->kgjnp/dot_general | solution.py:66
  369.3 0.3 convolution_bitcast_fusion
  369.6 0.0 copy-start
  369.6 6.1 %fusion.11 = f32[2,4,32,64,128]{4,3,2,1,0:T(8,128)} fusion(f32[2,4,32,128,64]{3,0,4,2,1:T(2,128)S(1)} %fusion.21, bf16[2,128,4,128,1]{3,1,0,2,4:T(8,128)(2,1)S(1)} %bitcast.95), kind=kOutput, calls=%fused_computation.18 | convolution fusion | flops 3221225472 | bytes 17039360 | tf_op jit(solution)/shard_map/ktgn,kgjnp->ktgjp/dot_general | solution.py:75
  375.7 0.0 copy-done
  375.7 19.8 %fusion = f32[2,4,32,64,128]{4,3,2,1,0:T(8,128)} fusion(bf16[2,128,4,32,64]{1,4,3,2,0:T(8,128)(2,1)S(1)} %copy-done, f32[4,32,2,128]{3,1,0,2:T(8,128)S(1)} %copy.76, f32[4,2,128,128]{3,2,0,1:T(8,128)S(1)} %convolution_bitcast_fusion, pred[128,128]{1,0:T(8,128)(4,1)S(1)} %iota_compare_fusion, f32[4,32,2,128]{3,1,2,0:T(8,128)S(1)} %reduce_window_sum.24), kind=kOutput, calls=%fused_computation.1 | convolution fusion | flops 3238002688 | bytes 13385728 | tf_op jit(solution)/shard_map/gjkts,ksgjp->ktgjp/dot_general | solution.py:55
  395.5 0.0 collective-permute-done.2
  395.5 14.2 %fusion.8 = f32[2,128,4,32,64]{1,4,3,2,0:T(8,128)} fusion(bf16[2,128,4,32,64]{1,4,3,2,0:T(8,128)(2,1)} %copy.77, f32[2,4,32,64,128]{4,3,2,1,0:T(8,128)} %fusion.11, f32[2,4,32,64,128]{4,3,2,1,0:T(8,128)} %fusion, f32[4,32]{1,0:T(4,128)S(1)} %mul.176, f32[4,16,128,64]{2,3,1,0:T(8,128)} %collective-permute-done.2, ...), kind=kOutput, calls=%fused_computation.12 | convolution fusion | flops 3239051264 | bytes 34079232 | tf_op jit(solution)/shard_map/ktgn,gjnp->ktgjp/dot_general | solution.py:114
  409.7 104.2 %all_to_all.19 = f32[2,128,8192]{1,2,0:T(8,128)} all-to-all(f32[2,128,8192]{1,2,0:T(8,128)} %bitcast.91), channel_id=1, replica_groups=mesh['fh'=8,'fl'=2,'tp'=2] {'tp'}, dimensions={0} | all-to-all | bytes 16777216 | tf_op jit(solution)/shard_map/all_to_all | solution.py:117
  513.9 9.0 %copy.123 = f32[128,16384]{1,0:T(8,128)} copy(f32[128,16384]{0,1:T(8,128)} %bitcast.92) | data formatting | bytes 16777216 | tf_op jit(solution)/shard_map/all_to_all | solution.py:117
  (17 shorter events, 0.2 us)
Async XLA Ops:
  6.5 7.2 %copy-start.4 = (bf16[4,4,2304]{2,1,0:T(4,128)(2,1)S(1)}, bf16[4,4,2304]{2,1,0:T(4,128)(2,1)}, u32[]{:S(2)}) copy-start(bf16[4,4,2304]{2,1,0:T(4,128)(2,1)} %param.9) | copy-start | bytes 221188
  6.5 7.2 %copy-start.9 = (f32[128]{0:T(128)S(1)}, f32[128]{0:T(128)}, u32[]{:S(2)}) copy-start(f32[128]{0:T(128)} %param.12) | copy-start | bytes 1540
  6.5 7.2 %copy-start.7 = (f32[128]{0:T(128)S(1)}, f32[128]{0:T(128)}, u32[]{:S(2)}) copy-start(f32[128]{0:T(128)} %param.11) | copy-start | bytes 1540
  6.5 7.2 %copy-start.5 = (bf16[128,256]{1,0:T(8,128)(2,1)S(1)}, bf16[128,256]{1,0:T(8,128)(2,1)}, u32[]{:S(2)}) copy-start(bf16[128,256]{1,0:T(8,128)(2,1)} %param.8) | copy-start | bytes 196612
  6.5 10.5 %copy-start.6 = (bf16[4,2304]{1,0:T(4,128)(2,1)S(1)}, bf16[4,2304]{1,0:T(4,128)(2,1)}, u32[]{:S(2)}) copy-start(bf16[4,2304]{1,0:T(4,128)(2,1)} %param.10) | copy-start | bytes 55300
  6.5 313.0 %all-gather.5.cloned.1.call-start = ((), (), s32[]{:S(2)}) async-start(), calls=%async_computation.1 | async-start | bytes 18874368 | tf_op jit(solution)/shard_map/all_gather | solution.py:94
  9.6 2.2 copy-start.2
  11.8 6.6 %collective-permute-start = (bf16[3,4,2304]{2,0,1:T(4,128)(2,1)S(1)}, bf16[3,4,2304]{2,0,1:T(4,128)(2,1)S(1)}, u32[]{:S(2)}, u32[]{:S(2)}) collective-permute-start(bf16[3,4,2304]{2,0,1:T(4,128)(2,1)S(1)} %slice.52), channel_id=1, source_target_pairs={{0,2},{2,4},{4,6},{6,8},{8,10},{10,12},{12,14},{14,16},{16,18},{18... | collective-permute-start | bytes 165896 | tf_op jit(solution)/shard_map/ppermute | solution.py:15
  68.4 2.0 copy-start.1
  68.4 24.4 %copy-start.8 = (f32[128]{0:T(128)S(1)}, f32[128]{0:T(128)}, u32[]{:S(2)}) copy-start(f32[128]{0:T(128)} %param.13) | copy-start | bytes 1540
  71.9 16.2 %collective-permute-start.1 = (f32[4,16,128,64]{2,3,1,0:T(8,128)}, f32[4,16,128,64]{2,3,1,0:T(8,128)S(1)}, u32[]{:S(2)}, u32[]{:S(2)}) collective-permute-start(f32[4,16,128,64]{2,3,1,0:T(8,128)} %constant_dynamic-slice_fusion), channel_id=1, source_target_pairs={{0,2},{2,0},{1,3},{3,1},{4,6},{6,4},{5,7},{7,5},{8,10},{10,8},{9,1... | collective-permute-start | bytes 6291464 | tf_op jit(solution)/shard_map/ppermute | solution.py:88
  88.1 239.8 %copy-start.3 = (f32[4,16,128,64]{2,3,1,0:T(8,128)}, f32[4,16,128,64]{2,3,1,0:T(8,128)S(1)}, u32[]{:S(2)}) copy-start(f32[4,16,128,64]{2,3,1,0:T(8,128)S(1)} %collective-permute-done.1) | copy-start | bytes 6291460
  331.3 64.2 %collective-permute-start.2 = (f32[4,16,128,64]{2,3,1,0:T(8,128)S(1)}, f32[4,16,128,64]{2,3,1,0:T(8,128)}, u32[]{:S(2)}, u32[]{:S(2)}) collective-permute-start(f32[4,16,128,64]{2,3,1,0:T(8,128)S(1)} %get-tuple-element.8), channel_id=1, source_target_pairs={{0,2},{2,0},{1,3},{3,1},{4,6},{6,4},{5,7},{7,5},{8,10},{10,8},{9,1... | collective-permute-start | bytes 6291464 | tf_op jit(solution)/shard_map/ppermute | solution.py:107
  369.6 6.1 %copy-start = (bf16[2,128,4,32,64]{1,4,3,2,0:T(8,128)(2,1)S(1)}, bf16[2,128,4,32,64]{1,4,3,2,0:T(8,128)(2,1)}, u32[]{:S(2)}) copy-start(bf16[2,128,4,32,64]{1,4,3,2,0:T(8,128)(2,1)} %copy.77) | copy-start | bytes 12582916
Sparse Core Ops, SparseCore 0:
  92.3 227.1 all-gather.4

commit v2 on v1

--- a/solution.py
+++ b/solution.py
@@ -22,7 +22,7 @@
     return jax.nn.silu(summed).astype(jnp.bfloat16)
 
 
-def shards(xbc, dt_raw, conv_weight, conv_bias, dt_bias, a_log, d_skip, seq_count):
+def shards(xbc, dt_raw, conv_weight, conv_bias, dt_bias, a_log, d_skip, seq_count, tp_count):
     row_count, group_count, _ = xbc.shape
     head_count = dt_raw.shape[0]
     per_group = head_count // group_count
@@ -61,7 +61,7 @@
 
     kk = jnp.arange(nck)
     between = (kk[None, :, None] < kk[None, None, :]) & (kk[None, None, :] < kk[:, None, None])
-    gap_log = jnp.einsum("kam,gjm->gjka", between.astype(f32), chunk_log)
+    gap_log = jnp.einsum("kam,gjm->gjka", between.astype(f32), chunk_log, precision=exact)
     pre_w = jnp.where((kk[None, :] < kk[:, None])[None, None], jnp.exp(gap_log), 0.0)
     local_in = jnp.einsum("gjka,agjnp->kgjnp", pre_w, chunk_states, precision=exact)
     cum_dev = cum + jnp.concatenate(
@@ -69,7 +69,7 @@
     )[..., None]
     dev_log = jnp.sum(chunk_log, axis=2)
     later = (kk[:, None] < kk[None, :]).astype(f32)
-    after_w = jnp.exp(jnp.einsum("km,gjm->gjk", later, chunk_log))
+    after_w = jnp.exp(jnp.einsum("km,gjm->gjk", later, chunk_log, precision=exact))
     dev_state = jnp.einsum("gjk,kgjnp->gjnp", after_w, chunk_states, precision=exact)
 
     carried_local = jnp.einsum("ktgn,kgjnp->ktgjp", c_part.astype(f32), local_in, precision=exact)
@@ -79,27 +79,20 @@
     hi = lax.axis_index("fh")
     pair_count = seq_count // 2
     half = per_group // 2
-    all_log = lax.all_gather(dev_log, SEQ)
-    first_log = all_log[2 * hi]
-    second_log = all_log[2 * hi + 1]
+    swap = [(0, 1), (1, 0)]
+    partner_log = lax.ppermute(dev_log, "fl", swap)
+    first_log = jnp.where(lo == 0, dev_log, partner_log)
+    second_log = jnp.where(lo == 0, partner_log, dev_log)
     own_half = lax.dynamic_slice_in_dim(dev_state, lo * half, half, axis=1)
     other_half = lax.dynamic_slice_in_dim(dev_state, (1 - lo) * half, half, axis=1)
-    swap = [(0, 1), (1, 0)]
     recv_a = lax.ppermute(other_half, "fl", swap)
     first_state = jnp.where(lo == 0, own_half, recv_a)
     second_state = jnp.where(lo == 0, recv_a, own_half)
     second_log_half = lax.dynamic_slice_in_dim(second_log, lo * half, half, axis=1)
     first_log_half = lax.dynamic_slice_in_dim(first_log, lo * half, half, axis=1)
     pair_state = jnp.exp(second_log_half)[..., None, None] * first_state + second_state
-    gathered = lax.all_gather(pair_state, "fh")
-
-    pair_log = all_log.reshape(pair_count, 2, group_count, per_group).sum(axis=1)
-    pair_log_half = lax.dynamic_slice_in_dim(pair_log, lo * half, half, axis=2)
-    pp = jnp.arange(pair_count)
-    strictly = (pp[:, None] < pp[None, :]) & (pp[None, :] < hi)
-    gap = jnp.einsum("am,mgj->agj", strictly.astype(f32), pair_log_half)
-    pair_w = jnp.where((pp < hi)[:, None, None], jnp.exp(gap), 0.0)
-    pair_in = jnp.einsum("agj,agjnp->gjnp", pair_w, gathered, precision=exact)
+    pair_log_half = first_log_half + second_log_half
+    pair_in = exclusive_scan(pair_state, pair_log_half, hi, pair_count)
 
     first_decay = jnp.exp(first_log_half)[..., None, None]
     own_in = jnp.where(lo == 0, pair_in, first_decay * pair_in + recv_a)
@@ -113,8 +106,49 @@
 
     carried = jnp.einsum("ktgn,gjnp->ktgjp", c_part.astype(f32), incoming, precision=exact)
     output = output + jnp.transpose(jnp.exp(cum_dev), (2, 3, 0, 1))[..., None] * carried
-    merged = output.reshape(row_count, head_count * HEAD_DIM)
-    return lax.all_to_all(merged, "tp", split_axis=0, concat_axis=1, tiled=True)
+    return exchange_rows(output.reshape(row_count, head_count * HEAD_DIM), tp_count)
+
+
+def exclusive_scan(state, log_decay, mine, count):
+    def shifted(value, step):
+        return lax.ppermute(value, "fh", [(d, d + step) for d in range(count - step)])
+
+    def pack(st, lg):
+        return jnp.concatenate([st, jnp.broadcast_to(lg[..., None, None], st.shape[:2] + (1, st.shape[3]))], axis=2)
+
+    packed = shifted(pack(state, log_decay), 1)
+    cur_s, cur_a = packed[:, :, :STATE], packed[:, :, STATE, 0]
+    step = 1
+    while step < count:
+        got = shifted(pack(cur_s, cur_a), step)
+        take = mine >= step
+        new_s = jnp.exp(cur_a)[..., None, None] * got[:, :, :STATE] + cur_s
+        new_a = got[:, :, STATE, 0] + cur_a
+        cur_s = jnp.where(take, new_s, cur_s)
+        cur_a = jnp.where(take, new_a, cur_a)
+        step *= 2
+    return cur_s
+
+
+def exchange_rows(merged, tp_count):
+    mine = lax.axis_index("tp")
+    rows = merged.shape[0] // tp_count
+    blocks = merged.reshape(tp_count, rows, merged.shape[1])
+    pieces = [None] * tp_count
+    for shift in range(tp_count):
+        sent = lax.dynamic_index_in_dim(blocks, (mine + shift) % tp_count, 0, keepdims=False)
+        if shift == 0:
+            got = sent
+        else:
+            got = lax.ppermute(sent, "tp", [(d, (d + shift) % tp_count) for d in range(tp_count)])
+        pieces[shift] = got
+    placed = []
+    for column in range(tp_count):
+        value = pieces[0]
+        for shift in range(1, tp_count):
+            value = jnp.where((mine - shift) % tp_count == column, pieces[shift], value)
+        placed.append(value)
+    return jnp.concatenate(placed, axis=1)
 
 
 def solution(mesh):
@@ -133,6 +167,6 @@
     out_specs = P(SEQ + ("tp",), None)
 
     def body(*args):
-        return shards(*args, seq_count=seq_count)
+        return shards(*args, seq_count=seq_count, tp_count=tp_count)
 
     return jax.shard_map(body, mesh=grid, in_specs=in_specs, out_specs=out_specs, check_vma=False)

time: 535 us -> 767 us (1.43)
  waiting for transfers between devices: 228 us -> 550 us
  blocking collectives: 120 us -> 0 us
  other arithmetic: 32.3 us -> 46.2 us
  between operations: 13.7 us -> 0.66 us
  local copies, waits for them, and re-layouts: 45.3 us -> 57.4 us
  matrix products: 88.2 us -> 97.2 us
  starting transfers between devices: 2.32 us -> 11.3 us
    ppermute x0 -> x6, waiting for transfers between devices: none -> 549 us  [the longest x4 459 us: shifted(): lax.ppermute(value, 'fh', [(d, d + step) for d in range(count - step)])]
    all_gather x1 -> x0, waiting for transfers between devices: 227 us -> none  [shards(): gathered = lax.all_gather(pair_state, 'fh')]
    all_to_all x1 -> x0, blocking collectives: 104 us -> none  [shards(): return lax.all_to_all(merged, 'tp', split_axis=0, concat_axis=1, tiled=True)]
    dynamic_slice x1 -> x3, local copies, waits for them, and re-layouts: 0.08 us -> 18.5 us  [exchange_rows(): lax.dynamic_index_in_dim(blocks, (mine + shift) % tp_count, 0, keepdims=F...]
    all_gather x1 -> x0, blocking collectives: 15.8 us -> none  [shards(): all_log = lax.all_gather(dev_log, SEQ)]
    concatenate x0 -> x5, other arithmetic: none -> 11.6 us  [the longest x4 7.66 us: pack(): jnp.concatenate([st, jnp.broadcast_to(lg[..., None, None], st.shape[:2] +...]
    dot_general x1, matrix products: 19.8 us -> 29.1 us  [shards(): output = jnp.einsum('gjkts,ksgjp->ktgjp', mixing, values32, precision=exact)]
    all_to_all x1 -> x0, local copies, waits for them, and re-layouts: 8.99 us -> none  [shards(): return lax.all_to_all(merged, 'tp', split_axis=0, concat_axis=1, tiled=True)]
  transfers between devices with their start and end apart: 4 -> 9, of which waited for: 2 -> 7; matrix products, arithmetic and copies ran while one was open for 13% -> 11% of each run, Pallas kernels for 0% -> 0%
where the time goes in v2:
time: 767 us; the launch traced here: 763 us
  waiting for transfers between devices  550 us (72%)
  matrix products  97.2 us (13%)
  local copies, waits for them, and re-layouts  57.4 us (7%)
  other arithmetic  46.2 us (6%)
  starting transfers between devices  11.3 us (1%)
    ppermute x4, waiting for transfers between devices, shifted(): lax.ppermute(value, 'fh', [(d, d + step) for d in range(count - step)])  459 us
    ppermute x1, waiting for transfers between devices, exchange_rows(): lax.ppermute(sent, 'tp', [(d, (d + shift) % tp_count) for d in range(tp_c...  86.1 us
    dot_general x1, matrix products, shards(): jnp.einsum('gjka,agjnp->kgjnp', pre_w, chunk_states, precision=exact)  37.9 us
    dot_general x1, matrix products, shards(): output = jnp.einsum('gjkts,ksgjp->ktgjp', mixing, values32, precision=exact)  29.1 us
    reshape x2, local copies, waits for them, and re-layouts, shards(): activated[:, :, :inner_width]  24.3 us
    dynamic_slice x3, local copies, waits for them, and re-layouts, exchange_rows(): lax.dynamic_index_in_dim(blocks, (mine + shift) % tp_count, 0, keepdims=F...  18.5 us
  transfers between devices with their start and end apart: 9, of which 7 were waited for; matrix products, arithmetic and copies ran while one was open for 11% of the time, Pallas kernels for 0%

profile of v2, /device:TPU:24, one launch (start us, length us, event | category | flops | bytes accessed | tf_op | source)
XLA Modules:
  0.0 763.1 jit_solution(15324813215139092325)
XLA Ops:
  0.0 3.0 copy.72
  3.0 2.2 copy-done.2
  5.3 1.9 collective-permute-start
  7.3 0.2 compare_select_fusion
  7.5 2.3 reduce_window_sum.24
  9.8 0.2 slice_reduce_fusion.1
  10.0 0.1 copy.85
  10.2 0.1 fusion.46
  10.3 0.1 convolution_exponential_fusion.1
  10.5 1.3 collective-permute-done
  11.8 13.6 %multiply_convert_fusion = bf16[256,4,2304]{2,0,1:T(8,128)(2,1)S(1)} fusion(bf16[256,4,2304]{2,0,1:T(8,128)(2,1)} %copy-done.2, bf16[3,4,2304]{2,0,1:T(4,128)(2,1)S(1)} %collective-permute-done, f32[4,2304]{1,0:T(4,128)S(1)} %get-tuple-element.26, f32[4,2304]{1,0:T(4,128)S(1)} %get-tuple-element.27, f32[4,2304]{1,0:T(4,128)S(1)} %get-tuple-element.25, ...), kind=kLoop, calls=%fused_computation.8 | loop fusion | flops 61341696 | bytes 9676800 | tf_op jit(solution)/shard_map/convert_element_type | solution.py:22
  25.4 2.5 slice.85
  28.0 0.1 fusion.55
  28.1 12.9 %reshape.96 = bf16[2,128,4,32,64]{4,3,1,0,2:T(8,128)(2,1)} reshape(bf16[256,4,2048]{2,0,1:T(8,128)(2,1)} %slice.85) | data formatting | bytes 8388608 | tf_op jit(solution)/shard_map/reshape | solution.py:36
  40.9 11.5 %copy.82 = bf16[2,128,4,32,64]{1,4,3,2,0:T(8,128)(2,1)} copy(bf16[2,128,4,32,64]{4,3,1,0,2:T(8,128)(2,1)} %reshape.96) | data formatting | bytes 8388608 | tf_op jit(solution)/shard_map/reshape | solution.py:36
  52.4 9.5 %fusion.10 = (f32[4,32,128,64]{2,3,1,0:T(8,128)S(1)}, f32[2,4,32,64,128]{4,3,2,1,0:T(8,128)}) fusion(f32[4,32,2]{1,0,2:T(4,128)S(1)} %copy.123, bf16[2,128,4,128,1]{3,1,0,2,4:T(8,128)(2,1)S(1)} %bitcast.82, bf16[2,128,4,32,64]{1,4,3,2,0:T(8,128)(2,1)} %copy.82, f32[2,128,4,32]{1,3,0,2:T(8,128)S(1)} %fusion.46), kind=kOutput, calls=%fused_computation.16 | convolution fusion | flops 3228565504 | bytes 17171456 | tf_op jit(solution)/shard_map/ksgn,ksgjp->kgjnp/dot_general | solution.py:60
  61.9 1.9 copy-done.1
  63.9 1.4 constant_dynamic-slice_fusion.2
  65.3 0.3 collective-permute-start.2
  65.6 0.2 collective-permute-start.1
  65.8 3.9 collective-permute-done.1
  69.7 0.1 dynamic-slice_exponential_fusion.1
  69.8 2.7 select_add_fusion
  72.5 0.2 broadcast_in_dim.38
  72.7 0.4 pad_maximum_fusion.2
  73.2 2.8 collective-permute-start.3
  75.9 92.8 %collective-permute-done.3 = f32[4,16,129,64]{2,3,1,0:T(8,128)S(1)} collective-permute-done((f32[4,16,129,64]{2,3,1,0:T(8,128)S(1)}, f32[4,16,129,64]{2,3,1,0:T(8,128)S(1)}, u32[]{:S(2)}, u32[]{:S(2)}) %collective-permute-start.3) | collective-permute-done | bytes 2113568 | tf_op jit(solution)/shard_map/ppermute | solution.py:114
  168.7 0.3 exponential_reduce_fusion.2
  169.0 0.2 slice.91
  169.2 1.5 copy-done.5
  170.7 0.2 broadcast_in_dim.40
  170.9 2.4 pad_maximum_fusion.3
  173.3 1.9 collective-permute-start.4
  175.2 93.1 %collective-permute-done.4 = f32[4,16,129,64]{2,3,1,0:T(8,128)} collective-permute-done((f32[4,16,129,64]{2,3,1,0:T(8,128)}, f32[4,16,129,64]{2,3,1,0:T(8,128)}, u32[]{:S(2)}, u32[]{:S(2)}) %collective-permute-start.4) | collective-permute-done | bytes 2113568 | tf_op jit(solution)/shard_map/ppermute | solution.py:114
  268.3 1.4 exponential_reduce_fusion
  269.7 2.5 add_select_fusion.2
  272.2 0.2 broadcast_in_dim.42
  272.4 2.4 pad_maximum_fusion.4
  274.9 1.3 collective-permute-start.5
  276.2 92.0 %collective-permute-done.5 = f32[4,16,129,64]{2,3,1,0:T(8,128)} collective-permute-done((f32[4,16,129,64]{2,3,1,0:T(8,128)}, f32[4,16,129,64]{2,3,1,0:T(8,128)}, u32[]{:S(2)}, u32[]{:S(2)}) %collective-permute-start.5) | collective-permute-done | bytes 2113568 | tf_op jit(solution)/shard_map/ppermute | solution.py:114
  368.1 1.3 exponential_reduce_fusion.1
  369.4 1.9 add_select_fusion.1
  371.3 0.2 broadcast_in_dim.44
  371.6 2.4 pad_maximum_fusion.5
  374.0 1.3 collective-permute-start.6
  375.3 0.1 fusion.39
  375.5 0.1 copy.103
  375.7 0.1 mul.201
  375.8 0.1 bitcast_exponential_fusion
  375.9 181.2 %collective-permute-done.6 = f32[4,16,129,64]{2,3,1,0:T(8,128)} collective-permute-done((f32[4,16,129,64]{2,3,1,0:T(8,128)}, f32[4,16,129,64]{2,3,1,0:T(8,128)}, u32[]{:S(2)}, u32[]{:S(2)}) %collective-permute-start.6) | collective-permute-done | bytes 2113568 | tf_op jit(solution)/shard_map/ppermute | solution.py:114
  557.0 4.2 add_select_fusion.4
  561.2 0.1 collective-permute-start.7
  561.3 37.9 %fusion.21 = f32[2,4,32,128,64]{3,0,4,2,1:T(2,128)S(1)} fusion(f32[4,32,2,2,1]{3,2,4,1,0:T(2,128)S(1)} %copy.103, f32[2,4,32,128,64]{3,4,2,1,0:T(8,128)} %bitcast.76), kind=kOutput, calls=%fused_computation.30 | convolution fusion | flops 50331648 | bytes 16779264 | tf_op jit(solution)/shard_map/gjka,agjnp->kgjnp/dot_general | solution.py:66
  599.2 0.3 convolution_bitcast_fusion
  599.5 6.1 fusion.11
  605.6 29.1 %fusion = f32[2,4,32,64,128]{4,3,2,1,0:T(8,128)} fusion(bf16[2,128,4,32,64]{1,4,3,2,0:T(8,128)(2,1)S(1)} %copy-done, f32[4,32,2,128]{3,1,0,2:T(8,128)S(1)} %copy.81, f32[4,2,128,128]{3,2,0,1:T(8,128)S(1)} %convolution_bitcast_fusion, pred[128,128]{1,0:T(8,128)(4,1)S(1)} %iota_compare_fusion, f32[4,32,2,128]{3,1,2,0:T(8,128)S(1)} %reduce_window_sum.24), kind=kOutput, calls=%fused_computation | convolution fusion | flops 3238002688 | bytes 13385728 | tf_op jit(solution)/shard_map/gjkts,ksgjp->ktgjp/dot_general | solution.py:55
  634.7 14.1 %fusion.8 = f32[2,128,4,32,64]{1,4,3,2,0:T(8,128)} fusion(bf16[2,128,4,32,64]{1,4,3,2,0:T(8,128)(2,1)} %copy.82, f32[2,4,32,64,128]{4,3,2,1,0:T(8,128)} %fusion.11, f32[2,4,32,64,128]{4,3,2,1,0:T(8,128)} %fusion, f32[4,32]{1,0:T(4,128)S(1)} %mul.201, f32[4,16,128,64]{2,3,1,0:T(8,128)} %collective-permute-done.7, ...), kind=kOutput, calls=%fused_computation.11 | convolution fusion | flops 3239051264 | bytes 34079232 | tf_op jit(solution)/shard_map/ktgn,gjnp->ktgjp/dot_general | solution.py:107
  648.7 7.2 constant_dynamic-slice_fusion
  656.0 5.6 copy.99
  661.6 1.5 collective-permute-start.8
  663.1 5.6 copy.100
  668.7 86.1 %collective-permute-done.8 = f32[128,8192]{1,0:T(8,128)} collective-permute-done((f32[128,8192]{1,0:T(8,128)}, f32[128,8192]{1,0:T(8,128)}, u32[]{:S(2)}, u32[]{:S(2)}) %collective-permute-start.8) | collective-permute-done | bytes 4194336 | tf_op jit(solution)/shard_map/ppermute | solution.py:143
  754.8 4.0 bitcast_select_fusion.1
  758.9 4.0 pad_maximum_fusion
  (40 shorter events, 0.3 us)
Async XLA Ops:
  0.0 7.2 copy-start.6
  0.0 7.2 copy-start.11
  0.0 7.2 copy-start.9
  0.0 7.2 copy-start.7
  0.0 10.5 %copy-start.8 = (bf16[4,2304]{1,0:T(4,128)(2,1)S(1)}, bf16[4,2304]{1,0:T(4,128)(2,1)}, u32[]{:S(2)}) copy-start(bf16[4,2304]{1,0:T(4,128)(2,1)} %param.10) | copy-start | bytes 55300
  3.0 2.2 copy-start.2
  5.3 6.6 collective-permute-start
  61.9 1.9 copy-start.1
  65.3 4.5 collective-permute-start.2
  65.6 4.1 collective-permute-start.1
  69.8 2.9 copy-start.4
  73.2 95.6 %collective-permute-start.3 = (f32[4,16,129,64]{2,3,1,0:T(8,128)S(1)}, f32[4,16,129,64]{2,3,1,0:T(8,128)S(1)}, u32[]{:S(2)}, u32[]{:S(2)}) collective-permute-start(f32[4,16,129,64]{2,3,1,0:T(8,128)S(1)} %pad_maximum_fusion.2), channel_id=1, source_target_pairs={{0,4},{4,8},{8,12},{12,16},{16,20},{20,24},{24,28},{1,5},{5,9},{9,... | collective-permute-start | bytes 6340616 | tf_op jit(solution)/shard_map/ppermute | solution.py:114
  168.7 2.0 copy-start.5
  173.3 95.0 %collective-permute-start.4 = (f32[4,16,129,64]{2,3,1,0:T(8,128)}, f32[4,16,129,64]{2,3,1,0:T(8,128)}, u32[]{:S(2)}, u32[]{:S(2)}) collective-permute-start(f32[4,16,129,64]{2,3,1,0:T(8,128)} %pad_maximum_fusion.3), channel_id=1, source_target_pairs={{0,4},{4,8},{8,12},{12,16},{16,20},{20,24},{24,28},{1,5},{5,9},{9,... | collective-permute-start | bytes 6340616 | tf_op jit(solution)/shard_map/ppermute | solution.py:114
  274.9 93.3 %collective-permute-start.5 = (f32[4,16,129,64]{2,3,1,0:T(8,128)}, f32[4,16,129,64]{2,3,1,0:T(8,128)}, u32[]{:S(2)}, u32[]{:S(2)}) collective-permute-start(f32[4,16,129,64]{2,3,1,0:T(8,128)} %pad_maximum_fusion.4), channel_id=1, source_target_pairs={{0,8},{4,12},{8,16},{12,20},{16,24},{20,28},{1,9},{5,13},{9,17},{1... | collective-permute-start | bytes 6340616 | tf_op jit(solution)/shard_map/ppermute | solution.py:114
  371.3 2.6 copy-start.3
  371.5 4.1 copy-start.10
  374.0 183.1 %collective-permute-start.6 = (f32[4,16,129,64]{2,3,1,0:T(8,128)}, f32[4,16,129,64]{2,3,1,0:T(8,128)}, u32[]{:S(2)}, u32[]{:S(2)}) collective-permute-start(f32[4,16,129,64]{2,3,1,0:T(8,128)} %pad_maximum_fusion.5), channel_id=1, source_target_pairs={{0,16},{4,20},{8,24},{12,28},{1,17},{5,21},{9,25},{13,29},{2,18},{... | collective-permute-start | bytes 6340616 | tf_op jit(solution)/shard_map/ppermute | solution.py:114
  561.2 73.4 %collective-permute-start.7 = (f32[4,16,128,64]{2,3,1,0:T(8,128)S(1)}, f32[4,16,128,64]{2,3,1,0:T(8,128)}, u32[]{:S(2)}, u32[]{:S(2)}) collective-permute-start(f32[4,16,128,64]{2,3,1,0:T(8,128)S(1)} %get-tuple-element.17), channel_id=1, source_target_pairs={{0,2},{2,0},{1,3},{3,1},{4,6},{6,4},{5,7},{7,5},{8,10},{10,8},{9,1... | collective-permute-start | bytes 6291464 | tf_op jit(solution)/shard_map/ppermute | solution.py:100
  599.5 6.1 copy-start
  661.6 93.3 %collective-permute-start.8 = (f32[128,8192]{1,0:T(8,128)}, f32[128,8192]{1,0:T(8,128)}, u32[]{:S(2)}, u32[]{:S(2)}) collective-permute-start(f32[128,8192]{1,0:T(8,128)} %bitcast.81), channel_id=1, source_target_pairs={{0,1},{1,0},{2,3},{3,2},{4,5},{5,4},{6,7},{7,6},{8,9},{9,8},{10,11... | collective-permute-start | bytes 12582920 | tf_op jit(solution)/shard_map/ppermute | solution.py:143

commit v3 on v2

--- a/solution.py
+++ b/solution.py
@@ -44,36 +44,37 @@
     cum = jnp.cumsum(rates, axis=3)
     chunk_log = cum[..., -1]
 
-    causal = lax.broadcasted_iota(jnp.int32, (chunk, chunk), 0) >= lax.broadcasted_iota(
-        jnp.int32, (chunk, chunk), 1
-    )
-    scores = jnp.einsum("ktgn,ksgn->kgts", c_part, b_part, preferred_element_type=f32)
-    gaps = cum[..., :, None] - cum[..., None, :]
-    decays = jnp.exp(jnp.where(causal, gaps, -jnp.inf))
-    mixing = decays * jnp.transpose(scores, (1, 0, 2, 3))[:, None] * steps[..., None, :]
     values32 = values.astype(f32)
-    output = jnp.einsum("gjkts,ksgjp->ktgjp", mixing, values32, precision=exact)
-    output = output + d_skip.reshape(group_count, per_group)[None, None, :, :, None] * values32
-
     weights = jnp.exp(chunk_log[..., None] - cum) * steps
     weighted = values32 * jnp.transpose(weights, (2, 3, 0, 1))[..., None]
     chunk_states = jnp.einsum("ksgn,ksgjp->kgjnp", b_part.astype(f32), weighted, precision=exact)
 
-    kk = jnp.arange(nck)
-    between = (kk[None, :, None] < kk[None, None, :]) & (kk[None, None, :] < kk[:, None, None])
-    gap_log = jnp.einsum("kam,gjm->gjka", between.astype(f32), chunk_log, precision=exact)
-    pre_w = jnp.where((kk[None, :] < kk[:, None])[None, None], jnp.exp(gap_log), 0.0)
-    local_in = jnp.einsum("gjka,agjnp->kgjnp", pre_w, chunk_states, precision=exact)
+    running = jnp.zeros_like(chunk_states[0])
+    local_list = []
+    for k in range(nck):
+        local_list.append(running)
+        running = jnp.exp(chunk_log[:, :, k])[..., None, None] * running + chunk_states[k]
+    local_in = jnp.stack(local_list, axis=0)
+    dev_state = running
     cum_dev = cum + jnp.concatenate(
         [jnp.zeros_like(chunk_log[..., :1]), jnp.cumsum(chunk_log, axis=2)[..., :-1]], axis=2
     )[..., None]
     dev_log = jnp.sum(chunk_log, axis=2)
-    later = (kk[:, None] < kk[None, :]).astype(f32)
-    after_w = jnp.exp(jnp.einsum("km,gjm->gjk", later, chunk_log, precision=exact))
-    dev_state = jnp.einsum("gjk,kgjnp->gjnp", after_w, chunk_states, precision=exact)
 
-    carried_local = jnp.einsum("ktgn,kgjnp->ktgjp", c_part.astype(f32), local_in, precision=exact)
-    output = output + jnp.transpose(jnp.exp(cum), (2, 3, 0, 1))[..., None] * carried_local
+    def intra(side):
+        values32, b_part, c_part, local_in = side
+        causal = lax.broadcasted_iota(jnp.int32, (chunk, chunk), 0) >= lax.broadcasted_iota(
+            jnp.int32, (chunk, chunk), 1
+        )
+        scores = jnp.einsum("ktgn,ksgn->kgts", c_part, b_part, preferred_element_type=f32)
+        gaps = cum[..., :, None] - cum[..., None, :]
+        decays = jnp.exp(jnp.where(causal, gaps, -jnp.inf))
+        mixing = decays * jnp.transpose(scores, (1, 0, 2, 3))[:, None] * steps[..., None, :]
+        output = jnp.einsum("gjkts,ksgjp->ktgjp", mixing, values32, precision=exact)
+        output = output + d_skip.reshape(group_count, per_group)[None, None, :, :, None] * values32
+
+        carried_local = jnp.einsum("ktgn,kgjnp->ktgjp", c_part.astype(f32), local_in, precision=exact)
+        return output + jnp.transpose(jnp.exp(cum), (2, 3, 0, 1))[..., None] * carried_local
 
     lo = lax.axis_index("fl")
     hi = lax.axis_index("fh")
@@ -92,7 +93,9 @@
     first_log_half = lax.dynamic_slice_in_dim(first_log, lo * half, half, axis=1)
     pair_state = jnp.exp(second_log_half)[..., None, None] * first_state + second_state
     pair_log_half = first_log_half + second_log_half
-    pair_in = exclusive_scan(pair_state, pair_log_half, hi, pair_count)
+    pair_in, output = exclusive_scan(
+        pair_state, pair_log_half, hi, pair_count, (values32, b_part, c_part, local_in), intra
+    )
 
     first_decay = jnp.exp(first_log_half)[..., None, None]
     own_in = jnp.where(lo == 0, pair_in, first_decay * pair_in + recv_a)
@@ -109,25 +112,35 @@
     return exchange_rows(output.reshape(row_count, head_count * HEAD_DIM), tp_count)
 
 
-def exclusive_scan(state, log_decay, mine, count):
+def exclusive_scan(state, log_decay, mine, count, side, work):
+    shape = state.shape
+    width = 1024
+
     def shifted(value, step):
         return lax.ppermute(value, "fh", [(d, d + step) for d in range(count - step)])
 
     def pack(st, lg):
-        return jnp.concatenate([st, jnp.broadcast_to(lg[..., None, None], st.shape[:2] + (1, st.shape[3]))], axis=2)
+        flat_log = jnp.pad(lg.reshape(1, -1), ((0, 0), (0, width - lg.size)))
+        return jnp.concatenate([st.reshape(-1, width), flat_log], axis=0)
 
-    packed = shifted(pack(state, log_decay), 1)
-    cur_s, cur_a = packed[:, :, :STATE], packed[:, :, STATE, 0]
+    def unpack(packed):
+        return packed[:-1].reshape(shape), packed[-1, : log_decay.size].reshape(log_decay.shape)
+
+    first, side = lax.optimization_barrier((pack(state, log_decay), side))
+    got = shifted(first, 1)
+    done = work(side)
+    got, done = lax.optimization_barrier((got, done))
+    cur_s, cur_a = unpack(got)
     step = 1
     while step < count:
-        got = shifted(pack(cur_s, cur_a), step)
+        got_s, got_a = unpack(shifted(pack(cur_s, cur_a), step))
         take = mine >= step
-        new_s = jnp.exp(cur_a)[..., None, None] * got[:, :, :STATE] + cur_s
-        new_a = got[:, :, STATE, 0] + cur_a
+        new_s = jnp.exp(cur_a)[..., None, None] * got_s + cur_s
+        new_a = got_a + cur_a
         cur_s = jnp.where(take, new_s, cur_s)
         cur_a = jnp.where(take, new_a, cur_a)
         step *= 2
-    return cur_s
+    return cur_s, done
 
 
 def exchange_rows(merged, tp_count):

time: 767 us -> 534 us (0.70)
  waiting for transfers between devices: 550 us -> 269 us
  local copies, waits for them, and re-layouts: 57.4 us -> 107 us
  matrix products: 97.2 us -> 57.4 us
  other arithmetic: 46.2 us -> 79.3 us
    ppermute x4, waiting for transfers between devices: 459 us -> 175 us  [shifted(): lax.ppermute(value, 'fh', [(d, d + step) for d in range(count - step)])]
    dot_general x6 -> x3, matrix products: 73.6 us -> 43.8 us  [the longest x1 36.7 us: intra(): output = jnp.einsum('gjkts,ksgjp->ktgjp', mixing, values32, precision=exact)]
    convert_element_type x0 -> x2, local copies, waits for them, and re-layouts: none -> 19.5 us  [shards(): values32 = values.astype(f32)]
    add x0 -> x3, other arithmetic: none -> 15.5 us  [the longest x1 12.3 us: shards(): output + jnp.transpose(jnp.exp(cum_dev), (2, 3, 0, 1))[..., None] * carried]
    mul x3 -> x5, local copies, waits for them, and re-layouts: 0.17 us -> 14.5 us  [the longest x4 14.4 us: exclusive_scan(): new_s = jnp.exp(cur_a)[..., None, None] * got_s + cur_s]
    reshape x2 -> x12, local copies, waits for them, and re-layouts: 24.3 us -> 31.7 us  [the longest x8 25.8 us: unpack(): packed[:-1].reshape(shape)]
  transfers between devices with their start and end apart: 9 -> 9, of which waited for: 7 -> 8; matrix products, arithmetic and copies ran while one was open for 11% -> 15% of each run, Pallas kernels for 0% -> 0%
where the time goes in v3:
time: 534 us; the launch traced here: 524 us
  waiting for transfers between devices  269 us (50%)
  local copies, waits for them, and re-layouts  107 us (20%)
  other arithmetic  79.3 us (15%)
  matrix products  57.4 us (11%)
  starting transfers between devices  10.9 us (2%)
    ppermute x4, waiting for transfers between devices, shifted(): lax.ppermute(value, 'fh', [(d, d + step) for d in range(count - step)])  175 us
    ppermute x1, waiting for transfers between devices, exchange_rows(): lax.ppermute(sent, 'tp', [(d, (d + shift) % tp_count) for d in range(tp_c...  85.8 us
    dot_general x1, matrix products, intra(): output = jnp.einsum('gjkts,ksgjp->ktgjp', mixing, values32, precision=exact)  36.7 us
    reshape x8, local copies, waits for them, and re-layouts, unpack(): packed[:-1].reshape(shape)  25.8 us
    convert_element_type x2, local copies, waits for them, and re-layouts, shards(): values32 = values.astype(f32)  19.5 us
    dynamic_slice x3, local copies, waits for them, and re-layouts, exchange_rows(): lax.dynamic_index_in_dim(blocks, (mine + shift) % tp_count, 0, keepdims=F...  18.5 us
    mul x4, local copies, waits for them, and re-layouts, exclusive_scan(): new_s = jnp.exp(cur_a)[..., None, None] * got_s + cur_s  14.4 us
    convert_element_type x1, other arithmetic, convolve(): return jax.nn.silu(summed).astype(jnp.bfloat16)  13.6 us
  transfers between devices with their start and end apart: 9, of which 8 were waited for; matrix products, arithmetic and copies ran while one was open for 15% of the time, Pallas kernels for 0%

profile of v3, /device:TPU:24, one launch (start us, length us, event | category | flops | bytes accessed | tf_op | source)
XLA Modules:
  0.0 523.7 jit_solution(12401790577159391936)
XLA Ops:
  0.0 3.0 copy.22
  3.0 2.2 copy-done.4
  5.2 1.9 collective-permute-start.1
  7.5 2.3 reduce_window_sum.24
  10.5 1.3 collective-permute-done.1
  11.8 13.6 %multiply_convert_fusion = bf16[256,4,2304]{2,0,1:T(8,128)(2,1)S(1)} fusion(bf16[256,4,2304]{2,0,1:T(8,128)(2,1)} %copy-done.4, bf16[3,4,2304]{2,0,1:T(4,128)(2,1)S(1)} %collective-permute-done.1, f32[4,2304]{1,0:T(4,128)S(1)} %get-tuple-element.42, f32[4,2304]{1,0:T(4,128)S(1)} %get-tuple-element.43, f32[4,2304]{1,0:T(4,128)S(1)} %get-tuple-element.41, ...), kind=kLoop, calls=%fused_computation.6 | loop fusion | flops 61341696 | bytes 9676800 | tf_op jit(solution)/shard_map/convert_element_type | solution.py:22
  25.4 4.5 slice_convert_fusion
  30.1 8.8 %copy.25 = f32[256,4,2048]{0,2,1:T(8,128)} copy(f32[256,4,2048]{2,0,1:T(8,128)} %slice_convert_fusion) | data formatting | bytes 16777216 | tf_op jit(solution)/shard_map/convert_element_type | solution.py:47
  38.8 10.8 %reshape.117 = f32[2,128,4,32,64]{1,0,4,3,2:T(2,128)} reshape(f32[256,4,2048]{0,2,1:T(8,128)} %copy.25) | data formatting | bytes 16777216 | tf_op jit(solution)/shard_map/convert_element_type | solution.py:47
  49.6 5.7 %broadcast_multiply_fusion = f32[2,128,4,32,64]{1,0,4,3,2:T(2,128)S(1)} fusion(f32[2,128,4,32,64]{1,0,4,3,2:T(2,128)} %reshape.117, f32[2,128,4,32]{1,0,3,2:T(2,128)S(1)} %copy.28), kind=kLoop, calls=%fused_computation.42 | loop fusion | flops 2097152 | bytes 16908288 | tf_op jit(solution)/shard_map/mul | solution.py:49
  55.3 4.6 fusion.33
  59.9 0.7 fusion.23
  60.6 2.6 copy-done
  63.3 1.6 constant_dynamic-slice_fusion.2
  64.8 1.0 copy-done.1
  68.4 1.8 collective-permute-done
  70.4 2.5 slice_add_fusion
  72.9 4.2 stack.4
  77.1 2.0 select_add_fusion
  79.1 3.8 copy.31
  83.0 5.2 reshape.106
  88.1 1.9 select_maximum_fusion.3
  90.0 2.5 collective-permute-start.3
  92.9 6.7 %fusion.37 = f32[2,4,32,64,128]{4,3,2,1,0:T(8,128)S(1)} fusion(f32[2,4,32,128,64]{3,4,2,1,0:T(8,128)} %stack.4, bf16[2,128,4,128]{3,1,0,2:T(8,128)(2,1)S(1)} %bitcast.86), kind=kOutput, calls=%fused_computation.61 | convolution fusion | flops 3221225472 | bytes 17039360 | tf_op jit(solution)/shard_map/ktgn,kgjnp->ktgjp/dot_general | solution.py:76
  99.7 36.7 %fusion.7 = f32[2,128,4,32,64]{1,4,3,2,0:T(8,128)} fusion(f32[2,4,32,64,128]{4,3,2,1,0:T(8,128)S(1)} %fusion.37, f32[2,128,4,32,64]{1,0,4,3,2:T(2,128)S(1)} %bitcast.84, f32[4,32,2,128]{3,1,0,2:T(8,128)S(1)} %copy-done.11, f32[4,2,128,128]{3,2,0,1:T(8,128)S(1)} %convolution_bitcast_fusion, pred[128,128]{1,0:T(8,128)(4,1)S(1)} %copy-done.15, ...), kind=kOutput, calls=%fused_computation.11 | convolution fusion | flops 3246391296 | bytes 26100224 | tf_op jit(solution)/shard_map/gjkts,ksgjp->ktgjp/dot_general | solution.py:73
  136.4 4.9 collective-permute-done.3
  141.6 1.7 select_maximum_fusion.2
  143.3 1.9 collective-permute-start.4
  145.2 48.8 %collective-permute-done.4 = f32[513,1024]{1,0:T(8,128)} collective-permute-done((f32[513,1024]{1,0:T(8,128)}, f32[513,1024]{1,0:T(8,128)}, u32[]{:S(2)}, u32[]{:S(2)}) %collective-permute-start.4) | collective-permute-done | bytes 2101280 | tf_op jit(solution)/shard_map/ppermute | solution.py:120
  194.1 0.7 slice_reduce_fusion.1
  194.9 2.3 mul.244.clone
  197.2 4.9 mul.245
  202.1 5.1 add_select_fusion.4
  207.2 1.4 copy-done.5
  208.6 1.6 select_maximum_fusion.1
  210.2 1.3 collective-permute-start.5
  211.6 47.6 %collective-permute-done.5 = f32[513,1024]{1,0:T(8,128)} collective-permute-done((f32[513,1024]{1,0:T(8,128)}, f32[513,1024]{1,0:T(8,128)}, u32[]{:S(2)}, u32[]{:S(2)}) %collective-permute-start.5) | collective-permute-done | bytes 2101280 | tf_op jit(solution)/shard_map/ppermute | solution.py:120
  260.0 2.3 mul.248.clone
  262.3 4.9 mul.249
  267.2 5.1 add_select_fusion.3
  272.3 1.6 select_maximum_fusion
  273.9 1.3 collective-permute-start.6
  275.2 2.5 reshape.112
  277.7 4.0 copy.46
  281.7 2.5 reshape.111
  284.2 4.0 copy.45
  288.2 2.5 reshape.110
  290.7 3.8 copy.44
  294.6 73.9 %collective-permute-done.6 = f32[513,1024]{1,0:T(8,128)} collective-permute-done((f32[513,1024]{1,0:T(8,128)}, f32[513,1024]{1,0:T(8,128)}, u32[]{:S(2)}, u32[]{:S(2)}) %collective-permute-start.6) | collective-permute-done | bytes 2101280 | tf_op jit(solution)/shard_map/ppermute | solution.py:120
  368.4 1.7 slice.114
  370.2 2.6 reshape.109
  372.7 3.8 copy.43
  376.5 5.7 %add_select_fusion.6 = (f32[4,16,128,64]{2,3,1,0:T(8,128)S(1)}, f32[4,16,128,64]{2,3,1,0:T(8,128)S(1)}) fusion(f32[4,16,128,64]{2,3,1,0:T(8,128)} %copy-done.6, f32[4,16]{1,0:T(4,128)S(1)} %get-tuple-element.52, pred[]{:T(512)S(6)} %eq.21, f32[4,16,128,64]{2,3,1,0:T(8,128)} %copy.46, f32[4,16,128,64]{2,3,1,0:T(8,128)} %copy.45, f32[4,16]{1,0:T(4,128)S(1)} %exp.81, ...), kind=kLoop, calls=%fused_computation.56 | loop fusion | flops 6291456 | bytes 14681092 | tf_op jit(solution)/shard_map/jit(_where)/select_n | solution.py:101
  382.2 1.6 add_select_fusion.5
  383.9 4.5 collective-permute-done.7
  388.3 9.0 %fusion.25 = f32[4,32,64,2,128]{4,2,1,0,3:T(8,128)} fusion(f32[4,16,128,64]{2,3,1,0:T(8,128)} %collective-permute-done.7, f32[4,16,128,64]{2,3,1,0:T(8,128)S(1)} %get-tuple-element.19, pred[]{:T(512)S(6)} %eq.21, bf16[2,128,4,128,1]{3,1,0,2,4:T(8,128)(2,1)S(1)} %bitcast.87), kind=kOutput, calls=%fused_computation.32 | convolution fusion | flops 3224371200 | bytes 12845057 | tf_op jit(solution)/shard_map/ktgn,gjnp->ktgjp/dot_general | solution.py:110
  397.4 12.3 %fusion.6 = f32[2,128,4,32,64]{1,4,3,2,0:T(8,128)} fusion(f32[2,128,4,32,64]{1,4,3,2,0:T(8,128)} %fusion.7, f32[4,32,64,2,128]{4,2,1,0,3:T(8,128)} %fusion.25, f32[2,128,4,32]{1,3,0,2:T(8,128)S(1)} %get-tuple-element.36), kind=kLoop, calls=%fused_computation.9 | loop fusion | flops 4194304 | bytes 25296896 | tf_op jit(solution)/shard_map/add | solution.py:111
  409.7 7.3 %constant_dynamic-slice_fusion = (f32[1,128,8192]{1,2,0:T(8,128)}, f32[1,128,8192]{1,2,0:T(8,128)}) fusion(f32[2,128,8192]{1,2,0:T(8,128)} %bitcast.82, s32[]{:T(128)S(6)} %select_n.196, s32[]{:T(128)S(6)} %select_n.194), kind=kLoop, calls=%fused_computation.91 | loop fusion | bytes 16777224 | tf_op jit(solution)/shard_map/jit(dynamic_index_in_dim)/dynamic_slice | solution.py:152
  416.9 5.6 %copy.49 = f32[1,128,8192]{2,1,0:T(8,128)} copy(f32[1,128,8192]{1,2,0:T(8,128)} %get-tuple-element.24) | data formatting | bytes 8388608 | tf_op jit(solution)/shard_map/jit(dynamic_index_in_dim)/dynamic_slice | solution.py:152
  422.5 1.5 collective-permute-start.8
  424.1 5.6 %copy.50 = f32[1,128,8192]{2,1,0:T(8,128)} copy(f32[1,128,8192]{1,2,0:T(8,128)} %get-tuple-element.23) | data formatting | bytes 8388608 | tf_op jit(solution)/shard_map/jit(dynamic_index_in_dim)/dynamic_slice | solution.py:152
  429.7 85.8 %collective-permute-done.8 = f32[128,8192]{1,0:T(8,128)} collective-permute-done((f32[128,8192]{1,0:T(8,128)}, f32[128,8192]{1,0:T(8,128)}, u32[]{:S(2)}, u32[]{:S(2)}) %collective-permute-start.8) | collective-permute-done | bytes 4194336 | tf_op jit(solution)/shard_map/ppermute | solution.py:156
  515.5 4.0 bitcast_select_fusion.1
  519.5 4.0 pad_maximum_fusion
  (78 shorter events, 5.3 us)
Async XLA Ops:
  0.0 7.2 %copy-start.18 = (f32[128]{0:T(128)S(1)}, f32[128]{0:T(128)}, u32[]{:S(2)}) copy-start(f32[128]{0:T(128)} %param.12) | copy-start | bytes 1540
  0.0 7.2 %copy-start.13 = (bf16[128,256]{1,0:T(8,128)(2,1)S(1)}, bf16[128,256]{1,0:T(8,128)(2,1)}, u32[]{:S(2)}) copy-start(bf16[128,256]{1,0:T(8,128)(2,1)} %param.8) | copy-start | bytes 196612
  0.0 7.2 %copy-start.16 = (f32[128]{0:T(128)S(1)}, f32[128]{0:T(128)}, u32[]{:S(2)}) copy-start(f32[128]{0:T(128)} %param.11) | copy-start | bytes 1540
  0.0 10.0 %copy-start.12 = (bf16[4,4,2304]{2,1,0:T(4,128)(2,1)S(1)}, bf16[4,4,2304]{2,1,0:T(4,128)(2,1)}, u32[]{:S(2)}) copy-start(bf16[4,4,2304]{2,1,0:T(4,128)(2,1)} %param.9) | copy-start | bytes 221188
  0.0 10.3 %copy-start.14 = (bf16[4,2304]{1,0:T(4,128)(2,1)S(1)}, bf16[4,2304]{1,0:T(4,128)(2,1)}, u32[]{:S(2)}) copy-start(bf16[4,2304]{1,0:T(4,128)(2,1)} %param.10) | copy-start | bytes 55300
  3.0 2.2 copy-start.4
  5.2 6.6 %collective-permute-start.1 = (bf16[3,4,2304]{2,0,1:T(4,128)(2,1)S(1)}, bf16[3,4,2304]{2,0,1:T(4,128)(2,1)S(1)}, u32[]{:S(2)}, u32[]{:S(2)}) collective-permute-start(bf16[3,4,2304]{2,0,1:T(4,128)(2,1)S(1)} %slice.99), channel_id=1, source_target_pairs={{0,2},{2,4},{4,6},{6,8},{8,10},{10,12},{12,14},{14,16},{16,18},{18... | collective-permute-start | bytes 165896 | tf_op jit(solution)/shard_map/ppermute | solution.py:15
  59.9 3.3 copy-start
  63.2 2.6 copy-start.1
  63.2 5.1 copy-start.17
  65.8 11.3 %collective-permute-start.2 = (f32[4,16,128,64]{2,3,1,0:T(8,128)}, f32[4,16,128,64]{2,3,1,0:T(8,128)S(1)}, u32[]{:S(2)}, u32[]{:S(2)}) collective-permute-start(f32[4,16,128,64]{2,3,1,0:T(8,128)} %constant_dynamic-slice_fusion.2), channel_id=1, source_target_pairs={{0,2},{2,0},{1,3},{3,1},{4,6},{6,4},{5,7},{7,5},{8,10},{10,8},{9,1... | collective-permute-start | bytes 6291464 | tf_op jit(solution)/shard_map/ppermute | solution.py:89
  66.1 4.1 collective-permute-start
  72.9 4.2 copy-start.2
  77.1 5.8 %copy-start.6 = (f32[4,16,128,64]{2,3,1,0:T(8,128)}, f32[4,16,128,64]{2,3,1,0:T(8,128)S(1)}, u32[]{:S(2)}) copy-start(f32[4,16,128,64]{2,3,1,0:T(8,128)S(1)} %collective-permute-done.2) | copy-start | bytes 6291460
  88.1 11.5 %slice-start = ((s8[8388608]{0:T(1024)(128)(4,1)}), s8[4194304]{0:T(1024)(128)(4,1)S(1)}, s32[]{:S(2)}) async-start(s8[8388608]{0:T(1024)(128)(4,1)} %bitcast.83), calls=%async_computation | async-start | bytes 8388608
  90.0 51.3 %collective-permute-start.3 = (f32[513,1024]{1,0:T(8,128)S(1)}, f32[513,1024]{1,0:T(8,128)S(1)}, u32[]{:S(2)}, u32[]{:S(2)}) collective-permute-start(f32[513,1024]{1,0:T(8,128)S(1)} %select_maximum_fusion.3), channel_id=1, source_target_pairs={{0,4},{4,8},{8,12},{12,16},{16,20},{20,24},{24,28},{1,5},{5,9},{9,... | collective-permute-start | bytes 6303752 | tf_op jit(solution)/shard_map/ppermute | solution.py:120
  92.8 6.8 %slice-start.1 = ((s8[8388608]{0:T(1024)(128)(4,1)}), s8[4194304]{0:T(1024)(128)(4,1)S(1)}, s32[]{:S(2)}) async-start(s8[8388608]{0:T(1024)(128)(4,1)} %bitcast.83), calls=%async_computation.1 | async-start | bytes 8388608
  92.8 6.8 %copy-start.10 = (f32[2,128,4,32]{1,3,0,2:T(8,128)S(1)}, f32[2,128,4,32]{1,3,0,2:T(8,128)}, u32[]{:S(2)}) copy-start(f32[2,128,4,32]{1,3,0,2:T(8,128)} %get-tuple-element.37) | copy-start | bytes 393220
  92.8 6.8 %copy-start.11 = (f32[4,32,2,128]{3,1,0,2:T(8,128)S(1)}, f32[4,32,2,128]{3,1,0,2:T(8,128)}, u32[]{:S(2)}) copy-start(f32[4,32,2,128]{3,1,0,2:T(8,128)} %copy.34) | copy-start | bytes 393220
  92.9 6.8 %copy-start.15 = (pred[128,128]{1,0:T(8,128)(4,1)S(1)}, pred[128,128]{1,0:T(8,128)(4,1)}, u32[]{:S(2)}) copy-start(pred[128,128]{1,0:T(8,128)(4,1)} %iota_compare_fusion.1) | copy-start | bytes 49156
  141.3 2.0 copy-start.9
  143.3 50.8 %collective-permute-start.4 = (f32[513,1024]{1,0:T(8,128)}, f32[513,1024]{1,0:T(8,128)}, u32[]{:S(2)}, u32[]{:S(2)}) collective-permute-start(f32[513,1024]{1,0:T(8,128)} %select_maximum_fusion.2), channel_id=1, source_target_pairs={{0,4},{4,8},{8,12},{12,16},{16,20},{20,24},{24,28},{1,5},{5,9},{9,... | collective-permute-start | bytes 6303752 | tf_op jit(solution)/shard_map/ppermute | solution.py:120
  207.2 1.4 copy-start.5
  210.2 49.0 %collective-permute-start.5 = (f32[513,1024]{1,0:T(8,128)}, f32[513,1024]{1,0:T(8,128)}, u32[]{:S(2)}, u32[]{:S(2)}) collective-permute-start(f32[513,1024]{1,0:T(8,128)} %select_maximum_fusion.1), channel_id=1, source_target_pairs={{0,8},{4,12},{8,16},{12,20},{16,24},{20,28},{1,9},{5,13},{9,17},{1... | collective-permute-start | bytes 6303752 | tf_op jit(solution)/shard_map/ppermute | solution.py:120
  273.9 94.6 %collective-permute-start.6 = (f32[513,1024]{1,0:T(8,128)}, f32[513,1024]{1,0:T(8,128)}, u32[]{:S(2)}, u32[]{:S(2)}) collective-permute-start(f32[513,1024]{1,0:T(8,128)} %select_maximum_fusion), channel_id=1, source_target_pairs={{0,16},{4,20},{8,24},{12,28},{1,17},{5,21},{9,25},{13,29},{2,18},{... | collective-permute-start | bytes 6303752 | tf_op jit(solution)/shard_map/ppermute | solution.py:120
  277.7 4.0 copy-start.7
  284.2 4.0 copy-start.8
  376.5 5.7 %copy-start.3 = (f32[4,32,128,64]{2,3,1,0:T(8,128)S(1)}, f32[4,32,128,64]{2,3,1,0:T(8,128)}, u32[]{:S(2)}) copy-start(f32[4,32,128,64]{2,3,1,0:T(8,128)} %copy-done.1) | copy-start | bytes 12582916
  383.8 4.5 collective-permute-start.7
  422.5 92.9 %collective-permute-start.8 = (f32[128,8192]{1,0:T(8,128)}, f32[128,8192]{1,0:T(8,128)}, u32[]{:S(2)}, u32[]{:S(2)}) collective-permute-start(f32[128,8192]{1,0:T(8,128)} %bitcast.88), channel_id=1, source_target_pairs={{0,1},{1,0},{2,3},{3,2},{4,5},{5,4},{6,7},{7,6},{8,9},{9,8},{10,11... | collective-permute-start | bytes 12582920 | tf_op jit(solution)/shard_map/ppermute | solution.py:156
